TPU v7x, 256 devices: a whole 4x4x8 slice. The times are simulated.
256 devices in a mesh: wide: 32 (over z_hi, y, core), narrow: 8 (over z_lo, x).
Axes of the slice: x: 4, y: 4, z: 8 (z_hi: 4, z_lo: 2; z = z_hi * 2 + z_lo), core: 2. Of those that a mesh axis runs over, the one named last changes fastest.
Arguments:
- residual: bfloat16 [256, 8192], P('wide'), may hold values from -60 to 60
- norm_gain: float32 [8192], replicated, may hold values from 0.1 to 1.9
- w_query: bfloat16 [8192, 8192], P('wide', 'narrow'), may hold values from -0.0625 to 0.0625
- key_projection_weight: bfloat16 [8192, 1024], P('wide', 'narrow'), may hold values from -0.0625 to 0.0625
- value_projection_weight: bfloat16 [8192, 1024], P('wide', 'narrow'), may hold values from -0.0625 to 0.0625
- w_out: bfloat16 [8192, 8192], P('narrow', 'wide'), may hold values from -0.5 to 0.5
- cache_keys: bfloat16 [256, 8, 1024, 128], P('wide', 'narrow'), may hold values from -480 to 480
- stored_values: bfloat16 [256, 8, 1024, 128], P('wide', 'narrow'), may hold values from -24 to 24
- lengths: int32 [256], P('wide'), may hold values from 1 to 1024, as said below
- w_enc: bfloat16 [8192, 65536], P('narrow', 'wide'), may hold values from -0.0625 to 0.0625
- b_enc: float32 [65536], P('wide'), may hold values from -3 to 3
- w_dec: bfloat16 [65536, 8192], P('wide', 'narrow'), may hold values from -0.0625 to 0.0625
- b_dec: float32 [8192], P('narrow'), may hold values from -3 to 3
- clamp_index: int32 [256, 8], replicated, may hold values from 0 to 65535, as said below
- clamp_value: float32 [256, 8], replicated, may hold values from 10 to 40
Outputs:
- steered: bfloat16 [256, 8192], P('wide', 'narrow')
Inputs may be any that keep to these rules, and one draw needn't show every extreme that they name: `lengths`: row 0 has all 1024 slots filled. `clamp_index`: the 8 latents of a row are distinct.
All inputs are finite; a program needn't handle non-finite values.
Results may differ from a plain program's by a relative error of at most 0.014.
The roundings to bfloat16 on the way count: a program that leaves them out, or rounds other values in their place, can miss the bound.
Values may be sent and summed in bfloat16 or wider, within the bound.
No kernel may reach another device: no remote copies, remote signals or barrier semaphores. Data moves between devices by JAX's collectives and lax.ppermute only.
A program may use at most 64 MiB of HBM per device.

v0:
```python
import math
import jax
import jax.numpy as jnp
from jax import lax
from jax.sharding import PartitionSpec as P

HEAD_WIDTH = 128
rope_base = 500000.0


def rotary(vectors, positions):
    halfway = vectors.shape[-1] // 2
    counter = jnp.arange(halfway, dtype=jnp.float32)
    inverse = rope_base ** (-2.0 * counter / vectors.shape[-1])
    angles = positions.astype(jnp.float32)[:, None] * inverse[None, :]
    cosine = jnp.cos(angles)[:, None, :]
    sine = jnp.sin(angles)[:, None, :]
    first_half = vectors[..., :halfway]
    second_half = vectors[..., halfway:]
    return jnp.concatenate(
        [first_half * cosine - second_half * sine, second_half * cosine + first_half * sine],
        axis=-1,
    )


def clamp_latents(pre_acts, latent_first, clamp_index, clamp_value):
    columns = latent_first + jnp.arange(pre_acts.shape[1], dtype=jnp.int32)
    result = jnp.maximum(pre_acts, 0.0)
    for clamp_slot in range(clamp_index.shape[1]):
        matched = columns[None, :] == clamp_index[:, clamp_slot : clamp_slot + 1]
        result = jnp.where(matched, clamp_value[:, clamp_slot : clamp_slot + 1], result)
    return result.astype(jnp.bfloat16)


def attend(queries, key_new, value_new, cache_keys, stored_values, lengths):
    local_rows, heads_here, head_size = queries.shape
    kv_here = key_new.shape[1]
    query_group_width = heads_here // kv_here
    grouped_queries = queries.reshape(local_rows, kv_here, query_group_width, head_size)
    scaling = 1.0 / math.sqrt(head_size)
    scores = (
        jnp.einsum(
            "rkgd,rkjd->rkgj", grouped_queries, cache_keys, preferred_element_type=jnp.float32
        )
        * scaling
    )
    in_range = (
        jnp.arange(cache_keys.shape[2], dtype=jnp.int32)[None, None, None, :]
        < lengths[:, None, None, None]
    )
    scores = jnp.where(in_range, scores, -jnp.inf)
    own_score = (
        jnp.einsum("rkgd,rkd->rkg", grouped_queries, key_new, preferred_element_type=jnp.float32)
        * scaling
    )
    highest = jnp.maximum(jnp.max(scores, axis=-1), own_score)
    weights = jnp.exp(scores - highest[..., None])
    own_weight = jnp.exp(own_score - highest)
    denominator = jnp.sum(weights, axis=-1) + own_weight
    probabilities = (weights / denominator[..., None]).astype(jnp.bfloat16)
    own_prob = (own_weight / denominator).astype(jnp.bfloat16)
    blended = jnp.einsum(
        "rkgj,rkjd->rkgd", probabilities, stored_values, preferred_element_type=jnp.float32
    )
    blended = (
        blended
        + own_prob.astype(jnp.float32)[..., None] * value_new.astype(jnp.float32)[:, :, None, :]
    )
    return blended.astype(jnp.bfloat16).reshape(local_rows, heads_here * head_size)


def on_device(
    residual,
    norm_gain,
    w_query,
    key_projection_weight,
    value_projection_weight,
    w_out,
    cache_keys,
    stored_values,
    lengths,
    w_enc,
    b_enc,
    w_dec,
    b_dec,
    clamp_index,
    clamp_value,
):
    stream = residual.astype(jnp.float32)
    local_rows = residual.shape[0]
    normalized_rows = (
        stream
        * lax.rsqrt(jnp.mean(stream * stream, axis=-1, keepdims=True) + 1e-05)
        * norm_gain[None, :]
    ).astype(jnp.bfloat16)
    by_feature = lax.all_to_all(normalized_rows, "wide", split_axis=1, concat_axis=0, tiled=True)
    query_width = w_query.shape[1]
    key_width = key_projection_weight.shape[1]
    row_block = by_feature
    projected = lax.psum_scatter(
        jnp.concatenate(
            [
                jnp.dot(row_block, w_query, preferred_element_type=jnp.float32),
                jnp.dot(row_block, key_projection_weight, preferred_element_type=jnp.float32),
                jnp.dot(row_block, value_projection_weight, preferred_element_type=jnp.float32),
            ],
            axis=1,
        ),
        "wide",
        scatter_dimension=0,
        tiled=True,
    )
    heads_here = query_width // HEAD_WIDTH
    kv_here = key_width // HEAD_WIDTH
    queries = rotary(
        projected[:, :query_width].reshape(local_rows, heads_here, HEAD_WIDTH), lengths
    ).astype(jnp.bfloat16)
    key_new = rotary(
        projected[:, query_width : query_width + key_width].reshape(
            local_rows, kv_here, HEAD_WIDTH
        ),
        lengths,
    ).astype(jnp.bfloat16)
    value_new = (
        projected[:, query_width + key_width :]
        .reshape(local_rows, kv_here, HEAD_WIDTH)
        .astype(jnp.bfloat16)
    )
    attended = attend(queries, key_new, value_new, cache_keys, stored_values, lengths)
    partial_out = jnp.dot(
        lax.all_gather(attended, "wide", axis=0, tiled=True),
        w_out,
        preferred_element_type=jnp.float32,
    )
    by_row = lax.all_to_all(partial_out, "wide", split_axis=0, concat_axis=1, tiled=True)
    head_total = lax.psum_scatter(by_row, "narrow", scatter_dimension=1, tiled=True)
    width_here = w_enc.shape[0]
    narrow_index = lax.axis_index("narrow")
    own_stream = lax.dynamic_slice_in_dim(stream, narrow_index * width_here, width_here, 1)
    hidden = (own_stream + head_total).astype(jnp.bfloat16)
    partial_pre = jnp.dot(
        lax.all_gather(hidden, "wide", axis=0, tiled=True),
        w_enc,
        preferred_element_type=jnp.float32,
    )
    latents_here = w_enc.shape[1]
    latent_first = lax.axis_index("wide") * latents_here
    summed_pre = lax.psum(partial_pre, "narrow")
    activations = clamp_latents(summed_pre + b_enc[None, :], latent_first, clamp_index, clamp_value)
    row_block = activations
    rebuilt = lax.psum_scatter(
        jnp.dot(row_block, w_dec, preferred_element_type=jnp.float32),
        "wide",
        scatter_dimension=0,
        tiled=True,
    )
    return (rebuilt + b_dec[None, :]).astype(jnp.bfloat16)


def solution(mesh):
    placed = (
        P("wide", None),
        P(),
        P("wide", "narrow"),
        P("wide", "narrow"),
        P("wide", "narrow"),
        P("narrow", "wide"),
        P("wide", "narrow", None, None),
        P("wide", "narrow", None, None),
        P("wide"),
        P("narrow", "wide"),
        P("wide"),
        P("wide", "narrow"),
        P("narrow"),
        P(),
        P(),
    )
    return jax.shard_map(
        on_device, mesh=mesh, in_specs=placed, out_specs=P("wide", "narrow"), check_vma=False
    )
```

profile of v0, /device:TPU:2, one launch (start us, length us, event | category | flops | bytes accessed | tf_op | source)
XLA Modules:
  0.0 458.9 jit_solution(15226275381327403887)
XLA Ops:
  6.5 0.0 copy-start
  6.5 0.0 reduce-scatter.4.cloned.1.call-start
  6.5 1.2 multiply_reduce_fusion
  7.8 1.0 multiply_convert_fusion
  8.8 22.2 %all_to_all.38 = bf16[8,32,256]{2,0,1:T(8,128)(2,1)S(1)} all-to-all(bf16[8,32,256]{2,0,1:T(8,128)(2,1)S(1)} %bitcast.75), channel_id=1, replica_groups=mesh['wide'=32,'narrow'=8] {'wide'}, dimensions={1} | all-to-all | bytes 262144 | tf_op jit(solution)/shard_map/all_to_all | solution.py:96
  31.0 1.3 fusion.44
  32.4 0.0 copy-done.4
  32.4 0.2 fusion.40
  32.6 0.0 copy-done.5
  32.6 0.0 copy-start.9
  32.6 0.2 fusion.42
  32.8 1.2 pad_maximum_fusion
  34.0 0.0 reduce-scatter.4.cloned.1.call-update
  34.0 0.0 reduce-scatter.6.cloned.1.call-start
  34.0 0.0 copy-done.9
  34.1 0.1 iota_compare_fusion
  34.2 0.1 multiply_cosine_fusion.1
  34.3 85.1 %reduce-scatter.4.cloned.1.call-done = f32[8,1280]{1,0:T(8,128)} async-done(((f32[256,1280]{1,0:T(8,128)}), f32[8,1280]{1,0:T(8,128)}) %reduce-scatter.4.cloned.1.call-update) | async-done | bytes 40976 | tf_op jit(solution)/shard_map/reduce_scatter | solution.py:100
  119.4 0.9 slice_bitcast_fusion
  120.3 0.1 fusion.66
  120.4 0.7 slice_bitcast_fusion.1
  121.0 0.1 fusion.61
  121.2 0.1 maximum_bitcast_fusion
  121.3 0.2 fusion.56
  121.5 0.8 fusion.69
  122.2 0.2 fusion.39
  122.5 0.7 fusion.59
  123.1 0.4 fusion.16
  123.6 44.2 %all_gather.6 = bf16[256,1024]{1,0:T(8,128)(2,1)S(1)} all-gather(bf16[8,1024]{1,0:T(8,128)(2,1)S(1)} %bitcast.76), channel_id=1, replica_groups=mesh['wide'=32,'narrow'=8] {'wide'}, dimensions={0}, use_global_device_ids=true | all-gather | bytes 540672 | tf_op jit(solution)/shard_map/all_gather | solution.py:131
  167.8 0.3 convolution_bitcast_fusion
  168.1 17.8 %all_to_all.39 = f32[32,8,256]{2,1,0:T(8,128)} all-to-all(f32[32,8,256]{2,1,0:T(8,128)S(1)} %convolution_bitcast_fusion), channel_id=1, replica_groups=mesh['wide'=32,'narrow'=8] {'wide'}, dimensions={0} | all-to-all | bytes 524288 | tf_op jit(solution)/shard_map/all_to_all | solution.py:135
  185.9 0.0 reduce-scatter.6.cloned.1.call-update
  185.9 0.0 all-reduce.2.cloned.1.call-start
  186.0 33.6 %reduce-scatter.6.cloned.1.call-done = f32[8,1024]{1,0:T(8,128)} async-done(((f32[8,8192]{1,0:T(8,128)}), f32[8,1024]{1,0:T(8,128)}) %reduce-scatter.6.cloned.1.call-update) | async-done | bytes 32784 | tf_op jit(solution)/shard_map/reduce_scatter | solution.py:136
  219.6 0.8 add_convert_fusion.1
  220.4 46.2 %all_gather.7 = bf16[256,1024]{1,0:T(8,128)(2,1)S(1)} all-gather(bf16[8,1024]{1,0:T(8,128)(2,1)S(1)} %add_convert_fusion.1), channel_id=1, replica_groups=mesh['wide'=32,'narrow'=8] {'wide'}, dimensions={0}, use_global_device_ids=true | all-gather | bytes 540672 | tf_op jit(solution)/shard_map/all_gather | solution.py:142
  266.6 4.8 %fusion.70 = f32[256,2048]{1,0:T(8,128)} fusion(bf16[256,1024]{1,0:T(8,128)(2,1)S(1)} %all_gather.7, bf16[1024,2048]{1,0:T(8,128)(2,1)} %param.24), kind=kOutput, calls=%fused_computation.88 | convolution fusion | flops 1073741824 | bytes 6815744 | tf_op jit(solution)/shard_map/dot_general | solution.py:141
  271.4 0.0 all-reduce.2.cloned.1.call-update
  271.4 0.0 reduce-scatter.8.cloned.1.call-start
  271.5 0.6 copy-done.6
  272.1 0.0 copy-done.7
  272.1 82.1 %all-reduce.2.cloned.1.call-done = f32[256,2048]{1,0:T(8,128)} async-done(((f32[256,2048]{1,0:T(8,128)}), f32[256,2048]{1,0:T(8,128)}) %all-reduce.2.cloned.1.call-update) | async-done | bytes 2097168 | tf_op jit(solution)/shard_map/psum | solution.py:148
  354.3 0.0 copy-done.10
  354.3 6.1 %fusion.19 = f32[256,1024]{1,0:T(8,128)} fusion(bf16[2048,1024]{1,0:T(8,128)(2,1)} %param.26, f32[256,2048]{1,0:T(8,128)} %all-reduce.2.cloned.1.call-done, f32[2048]{0:T(1024)S(1)} %copy-done.10, f32[256]{0:T(256)S(1)} %bitcast.93, f32[256]{0:T(256)S(1)} %bitcast.94, f32[256]{0:T(256)S(1)} %bitcast.88, f32[256]{0:T(256)S(1)} %bitcast.89, ...), kind=kOutput, calls=%fused_computation.12 | convolution fusion | flops 1083179008 | bytes 7372800 | tf_op jit(solution)/shard_map/dot_general | solution.py:152
  360.4 0.0 reduce-scatter.8.cloned.1.call-update
  360.4 90.6 %reduce-scatter.8.cloned.1.call-done = f32[8,1024]{1,0:T(8,128)} async-done(((f32[256,1024]{1,0:T(8,128)}), f32[8,1024]{1,0:T(8,128)}) %reduce-scatter.8.cloned.1.call-update) | async-done | bytes 32784 | tf_op jit(solution)/shard_map/reduce_scatter | solution.py:151
  451.0 0.0 copy-done.8
  451.0 1.4 add_convert_fusion
  (24 shorter events, 0.1 us)
Async XLA Ops:
  6.5 114.9 %copy-start = (bf16[8,1,1024,128]{3,2,1,0:T(8,128)(2,1)S(1)}, bf16[8,1,1024,128]{3,2,1,0:T(8,128)(2,1)}, u32[]{:S(2)}) copy-start(bf16[8,1,1024,128]{3,2,1,0:T(8,128)(2,1)} %param.21) | copy-start | bytes 6291460
  6.5 25.8 %copy-start.4 = (bf16[256,128]{1,0:T(8,128)(2,1)S(1)}, bf16[256,128]{1,0:T(8,128)(2,1)}, u32[]{:S(2)}) copy-start(bf16[256,128]{1,0:T(8,128)(2,1)} %param.19) | copy-start | bytes 196612
  6.5 26.0 %copy-start.5 = (bf16[256,128]{1,0:T(8,128)(2,1)S(1)}, bf16[256,128]{1,0:T(8,128)(2,1)}, u32[]{:S(2)}) copy-start(bf16[256,128]{1,0:T(8,128)(2,1)} %param.18) | copy-start | bytes 196612
  6.5 112.8 %reduce-scatter.4.cloned.1.call-start = ((), (), s32[]{:S(2)}) async-start(), calls=%async_computation.5 | async-start | bytes 1351680 | tf_op jit(solution)/shard_map/reduce_scatter | solution.py:100
  32.6 1.5 copy-start.9
  34.0 185.6 %reduce-scatter.6.cloned.1.call-start = ((), (), s32[]{:S(2)}) async-start(), calls=%async_computation.6 | async-start | bytes 294912 | tf_op jit(solution)/shard_map/reduce_scatter | solution.py:136
  119.4 3.8 copy-start.1
  122.2 45.5 %copy-start.3 = (bf16[1024,256]{1,0:T(8,128)(2,1)S(1)}, bf16[1024,256]{1,0:T(8,128)(2,1)}, u32[]{:S(2)}) copy-start(bf16[1024,256]{1,0:T(8,128)(2,1)} %param.20) | copy-start | bytes 1572868
  123.1 62.8 %copy-start.2 = (bf16[8,8192]{1,0:T(8,128)(2,1)S(1)}, bf16[8,8192]{1,0:T(8,128)(2,1)}, u32[]{:S(2)}) copy-start(bf16[8,8192]{1,0:T(8,128)(2,1)} %param.15) | copy-start | bytes 393220
  185.9 168.4 %all-reduce.2.cloned.1.call-start = ((), (), s32[]{:S(2)}) async-start(), calls=%async_computation.7 | async-start | bytes 4194304 | tf_op jit(solution)/shard_map/psum | solution.py:148
  271.4 0.7 copy-start.6
  271.4 0.7 copy-start.7
  271.4 82.9 %copy-start.10 = (f32[2048]{0:T(1024)S(1)}, f32[2048]{0:T(1024)}, u32[]{:S(2)}) copy-start(f32[2048]{0:T(1024)} %param.25) | copy-start | bytes 24580
  271.4 179.6 %reduce-scatter.8.cloned.1.call-start = ((), (), s32[]{:S(2)}) async-start(), calls=%async_computation.8 | async-start | bytes 1081344 | tf_op jit(solution)/shard_map/reduce_scatter | solution.py:151
  354.3 96.7 %copy-start.8 = (f32[1024]{0:T(1024)S(1)}, f32[1024]{0:T(1024)}, u32[]{:S(2)}) copy-start(f32[1024]{0:T(1024)} %param.27) | copy-start | bytes 12292
Sparse Core Ops, SparseCore 0:
  34.1 85.2 reduce-scatter.3
  186.0 33.5 reduce-scatter.5
  271.5 82.6 all-reduce.1
  360.5 90.4 reduce-scatter.7
where the time goes:
time: 459 us
  waiting for transfers between devices  292 us (64%)
  blocking collectives  130 us (28%)
  matrix products  14.3 us (3%)
  between operations  13.3 us (3%)
  other arithmetic  6.94 us (2%)
    reduce_scatter x1, waiting for transfers between devices, on_device(): lax.psum_scatter(jnp.dot(row_block, w_dec, preferred_element_type=jnp.flo...  90.6 us
    reduce_scatter x1, waiting for transfers between devices, on_device(): lax.psum_scatter(jnp.concatenate([jnp.dot(row_block, w_query, preferred_e...  85.1 us
    psum x1, waiting for transfers between devices, on_device(): summed_pre = lax.psum(partial_pre, 'narrow')  82.1 us
    all_gather x1, blocking collectives, on_device(): lax.all_gather(hidden, 'wide', axis=0, tiled=True)  46.2 us
    all_gather x1, blocking collectives, on_device(): lax.all_gather(attended, 'wide', axis=0, tiled=True)  44.2 us
    reduce_scatter x1, waiting for transfers between devices, on_device(): lax.psum_scatter(by_row, 'narrow', scatter_dimension=1, tiled=True)  33.6 us
    all_to_all x1, blocking collectives, on_device(): lax.all_to_all(normalized_rows, 'wide', split_axis=1, concat_axis=0, tile...  22.2 us
    all_to_all x1, blocking collectives, on_device(): lax.all_to_all(partial_out, 'wide', split_axis=0, concat_axis=1, tiled=True)  17.8 us
  transfers between devices with their start and end apart: 4, of which 4 were waited for; matrix products, arithmetic and copies ran while one was open for 0% of the time, Pallas kernels for 0%

commit v1 on v0

--- a/solution.py
+++ b/solution.py
@@ -3,9 +3,16 @@
 import jax.numpy as jnp
 from jax import lax
 from jax.sharding import PartitionSpec as P
+from jax.lax import all_to_all, axis_size
 
 HEAD_WIDTH = 128
 rope_base = 500000.0
+_advance_arrays = lambda which_axis, page: jnp.concatenate(
+    all_to_all(
+        jnp.stack([page] * axis_size(which_axis)), axis_name=which_axis, split_axis=0, concat_axis=0
+    ),
+    0,
+)
 
 
 def rotary(vectors, positions):
@@ -139,9 +146,7 @@
     own_stream = lax.dynamic_slice_in_dim(stream, narrow_index * width_here, width_here, 1)
     hidden = (own_stream + head_total).astype(jnp.bfloat16)
     partial_pre = jnp.dot(
-        lax.all_gather(hidden, "wide", axis=0, tiled=True),
-        w_enc,
-        preferred_element_type=jnp.float32,
+        _advance_arrays("wide", hidden), w_enc, preferred_element_type=jnp.float32
     )
     latents_here = w_enc.shape[1]
     latent_first = lax.axis_index("wide") * latents_here

time: 459 us -> 442 us (0.963)
  blocking collectives: 130 us -> 110 us
    all_gather x1 -> x0, blocking collectives: 46.2 us -> none  [on_device(): lax.all_gather(hidden, 'wide', axis=0, tiled=True)]
    all_to_all x0 -> x1, blocking collectives: none -> 26.3 us  [all_to_all(jnp.stack([page] * axis_size(which_axis)), axis_name=which_axi...]
where the time goes in v1:
time: 442 us; the launch traced here: 441 us
  waiting for transfers between devices  294 us (67%)
  blocking collectives  110 us (25%)
  matrix products  14.3 us (3%)
  between operations  13.3 us (3%)
  other arithmetic  6.94 us (2%)
    reduce_scatter x1, waiting for transfers between devices, on_device(): lax.psum_scatter(jnp.dot(row_block, w_dec, preferred_element_type=jnp.flo...  90.6 us
    reduce_scatter x1, waiting for transfers between devices, on_device(): lax.psum_scatter(jnp.concatenate([jnp.dot(row_block, w_query, preferred_e...  85.1 us
    psum x1, waiting for transfers between devices, on_device(): summed_pre = lax.psum(partial_pre, 'narrow')  84.3 us
    all_gather x1, blocking collectives, on_device(): lax.all_gather(attended, 'wide', axis=0, tiled=True)  44.2 us
    reduce_scatter x1, waiting for transfers between devices, on_device(): lax.psum_scatter(by_row, 'narrow', scatter_dimension=1, tiled=True)  33.6 us
    all_to_all x1, blocking collectives, all_to_all(jnp.stack([page] * axis_size(which_axis)), axis_name=which_axi...  26.3 us
    all_to_all x1, blocking collectives, on_device(): lax.all_to_all(normalized_rows, 'wide', split_axis=1, concat_axis=0, tile...  22.2 us
    all_to_all x1, blocking collectives, on_device(): lax.all_to_all(partial_out, 'wide', split_axis=0, concat_axis=1, tiled=True)  17.8 us
  transfers between devices with their start and end apart: 4, of which 4 were waited for; matrix products, arithmetic and copies ran while one was open for 0% of the time, Pallas kernels for 0%

profile of v1, /device:TPU:2, one launch (start us, length us, event | category | flops | bytes accessed | tf_op | source)
XLA Modules:
  0.0 441.2 jit_solution(5071816154270145934)
XLA Ops:
  6.5 0.0 copy-start
  6.5 0.0 reduce-scatter.4.cloned.1.call-start
  6.5 1.2 multiply_reduce_fusion
  7.8 1.0 multiply_convert_fusion
  8.8 22.2 %all_to_all.43 = bf16[8,32,256]{2,0,1:T(8,128)(2,1)S(1)} all-to-all(bf16[8,32,256]{2,0,1:T(8,128)(2,1)S(1)} %bitcast.77), channel_id=1, replica_groups=mesh['wide'=32,'narrow'=8] {'wide'}, dimensions={1} | all-to-all | bytes 262144 | tf_op jit(solution)/shard_map/all_to_all | solution.py:103
  31.0 1.3 fusion.46
  32.4 0.0 copy-done.4
  32.4 0.2 fusion.42
  32.6 0.0 copy-start.9
  32.6 0.2 fusion.44
  32.8 1.2 pad_maximum_fusion
  34.0 0.0 reduce-scatter.4.cloned.1.call-update
  34.0 0.0 reduce-scatter.6.cloned.1.call-start
  34.0 0.0 copy-done.9
  34.1 0.1 iota_compare_fusion
  34.2 0.1 multiply_cosine_fusion.1
  34.3 85.1 %reduce-scatter.4.cloned.1.call-done = f32[8,1280]{1,0:T(8,128)} async-done(((f32[256,1280]{1,0:T(8,128)}), f32[8,1280]{1,0:T(8,128)}) %reduce-scatter.4.cloned.1.call-update) | async-done | bytes 40976 | tf_op jit(solution)/shard_map/reduce_scatter | solution.py:107
  119.4 0.9 slice_bitcast_fusion
  120.3 0.1 fusion.68
  120.4 0.7 slice_bitcast_fusion.1
  121.0 0.1 fusion.63
  121.2 0.1 maximum_bitcast_fusion
  121.3 0.2 fusion.58
  121.5 0.8 fusion.71
  122.2 0.2 fusion.41
  122.5 0.7 fusion.61
  123.1 0.4 fusion.16
  123.6 44.2 %all_gather.3 = bf16[256,1024]{1,0:T(8,128)(2,1)S(1)} all-gather(bf16[8,1024]{1,0:T(8,128)(2,1)S(1)} %bitcast.78), channel_id=1, replica_groups=mesh['wide'=32,'narrow'=8] {'wide'}, dimensions={0}, use_global_device_ids=true | all-gather | bytes 540672 | tf_op jit(solution)/shard_map/all_gather | solution.py:138
  167.8 0.3 convolution_bitcast_fusion
  168.1 17.8 %all_to_all.44 = f32[32,8,256]{2,1,0:T(8,128)} all-to-all(f32[32,8,256]{2,1,0:T(8,128)S(1)} %convolution_bitcast_fusion), channel_id=1, replica_groups=mesh['wide'=32,'narrow'=8] {'wide'}, dimensions={0} | all-to-all | bytes 524288 | tf_op jit(solution)/shard_map/all_to_all | solution.py:142
  185.9 0.0 reduce-scatter.6.cloned.1.call-update
  185.9 0.0 all-reduce.2.cloned.1.call-start
  186.0 33.6 %reduce-scatter.6.cloned.1.call-done = f32[8,1024]{1,0:T(8,128)} async-done(((f32[8,8192]{1,0:T(8,128)}), f32[8,1024]{1,0:T(8,128)}) %reduce-scatter.6.cloned.1.call-update) | async-done | bytes 32784 | tf_op jit(solution)/shard_map/reduce_scatter | solution.py:143
  219.6 0.8 add_convert_fusion.1
  220.4 0.1 stack.2
  220.4 26.3 %all_to_all.45 = bf16[32,8,1024]{2,1,0:T(8,128)(2,1)S(1)} all-to-all(bf16[32,8,1024]{2,1,0:T(8,128)(2,1)S(1)} %stack.2), channel_id=1, replica_groups=mesh['wide'=32,'narrow'=8] {'wide'}, dimensions={0} | all-to-all | bytes 1048576 | tf_op jit(solution)/shard_map/all_to_all | solution.py:11
  246.7 4.8 %fusion.39 = f32[256,2048]{1,0:T(8,128)} fusion(bf16[1024,2048]{1,0:T(8,128)(2,1)} %param.24, bf16[32,8,1024]{2,1,0:T(8,128)(2,1)S(1)} %all_to_all.45), kind=kOutput, calls=%fused_computation.32 | convolution fusion | flops 1073741824 | bytes 6815744 | tf_op jit(solution)/shard_map/dot_general | solution.py:148
  251.5 0.0 all-reduce.2.cloned.1.call-update
  251.5 0.0 reduce-scatter.8.cloned.1.call-start
  251.6 0.6 copy-done.6
  252.2 0.0 copy-done.7
  252.2 84.3 %all-reduce.2.cloned.1.call-done = f32[256,2048]{1,0:T(8,128)} async-done(((f32[256,2048]{1,0:T(8,128)}), f32[256,2048]{1,0:T(8,128)}) %all-reduce.2.cloned.1.call-update) | async-done | bytes 2097168 | tf_op jit(solution)/shard_map/psum | solution.py:153
  336.6 0.0 copy-done.10
  336.6 6.1 %fusion.19 = f32[256,1024]{1,0:T(8,128)} fusion(bf16[2048,1024]{1,0:T(8,128)(2,1)} %param.26, f32[256,2048]{1,0:T(8,128)} %all-reduce.2.cloned.1.call-done, f32[2048]{0:T(1024)S(1)} %copy-done.10, f32[256]{0:T(256)S(1)} %bitcast.95, f32[256]{0:T(256)S(1)} %bitcast.96, f32[256]{0:T(256)S(1)} %bitcast.90, f32[256]{0:T(256)S(1)} %bitcast.91, ...), kind=kOutput, calls=%fused_computation.12 | convolution fusion | flops 1083179008 | bytes 7372800 | tf_op jit(solution)/shard_map/dot_general | solution.py:157
  342.7 0.0 reduce-scatter.8.cloned.1.call-update
  342.7 90.6 %reduce-scatter.8.cloned.1.call-done = f32[8,1024]{1,0:T(8,128)} async-done(((f32[256,1024]{1,0:T(8,128)}), f32[8,1024]{1,0:T(8,128)}) %reduce-scatter.8.cloned.1.call-update) | async-done | bytes 32784 | tf_op jit(solution)/shard_map/reduce_scatter | solution.py:156
  433.3 0.0 copy-done.8
  433.3 1.4 add_convert_fusion
  (25 shorter events, 0.1 us)
Async XLA Ops:
  6.5 114.9 %copy-start = (bf16[8,1,1024,128]{3,2,1,0:T(8,128)(2,1)S(1)}, bf16[8,1,1024,128]{3,2,1,0:T(8,128)(2,1)}, u32[]{:S(2)}) copy-start(bf16[8,1,1024,128]{3,2,1,0:T(8,128)(2,1)} %param.21) | copy-start | bytes 6291460
  6.5 25.8 %copy-start.4 = (bf16[256,128]{1,0:T(8,128)(2,1)S(1)}, bf16[256,128]{1,0:T(8,128)(2,1)}, u32[]{:S(2)}) copy-start(bf16[256,128]{1,0:T(8,128)(2,1)} %param.19) | copy-start | bytes 196612
  6.5 26.0 %copy-start.5 = (bf16[256,128]{1,0:T(8,128)(2,1)S(1)}, bf16[256,128]{1,0:T(8,128)(2,1)}, u32[]{:S(2)}) copy-start(bf16[256,128]{1,0:T(8,128)(2,1)} %param.18) | copy-start | bytes 196612
  6.5 112.8 %reduce-scatter.4.cloned.1.call-start = ((), (), s32[]{:S(2)}) async-start(), calls=%async_computation.6 | async-start | bytes 1351680 | tf_op jit(solution)/shard_map/reduce_scatter | solution.py:107
  32.6 1.5 copy-start.9
  34.0 185.6 %reduce-scatter.6.cloned.1.call-start = ((), (), s32[]{:S(2)}) async-start(), calls=%async_computation.7 | async-start | bytes 294912 | tf_op jit(solution)/shard_map/reduce_scatter | solution.py:143
  119.4 3.8 copy-start.1
  122.2 45.5 %copy-start.3 = (bf16[1024,256]{1,0:T(8,128)(2,1)S(1)}, bf16[1024,256]{1,0:T(8,128)(2,1)}, u32[]{:S(2)}) copy-start(bf16[1024,256]{1,0:T(8,128)(2,1)} %param.20) | copy-start | bytes 1572868
  123.1 62.8 %copy-start.2 = (bf16[8,8192]{1,0:T(8,128)(2,1)S(1)}, bf16[8,8192]{1,0:T(8,128)(2,1)}, u32[]{:S(2)}) copy-start(bf16[8,8192]{1,0:T(8,128)(2,1)} %param.15) | copy-start | bytes 393220
  185.9 150.7 %all-reduce.2.cloned.1.call-start = ((), (), s32[]{:S(2)}) async-start(), calls=%async_computation.8 | async-start | bytes 4194304 | tf_op jit(solution)/shard_map/psum | solution.py:153
  251.5 0.7 copy-start.6
  251.5 0.7 copy-start.7
  251.5 85.1 %copy-start.10 = (f32[2048]{0:T(1024)S(1)}, f32[2048]{0:T(1024)}, u32[]{:S(2)}) copy-start(f32[2048]{0:T(1024)} %param.25) | copy-start | bytes 24580
  251.5 181.8 %reduce-scatter.8.cloned.1.call-start = ((), (), s32[]{:S(2)}) async-start(), calls=%async_computation.9 | async-start | bytes 1081344 | tf_op jit(solution)/shard_map/reduce_scatter | solution.py:156
  336.6 96.7 %copy-start.8 = (f32[1024]{0:T(1024)S(1)}, f32[1024]{0:T(1024)}, u32[]{:S(2)}) copy-start(f32[1024]{0:T(1024)} %param.27) | copy-start | bytes 12292
Sparse Core Ops, SparseCore 0:
  34.1 85.2 reduce-scatter.3
  186.0 33.5 reduce-scatter.5
  251.7 84.8 all-reduce.1
  342.9 90.3 reduce-scatter.7
